TPU v7x, 32 devices: a whole 2x2x4 slice. The times are simulated.
32 devices in a mesh: lay: 4 (over y, x), slab: 8 (over z, core).
Axes of the slice: x: 2, y: 2, z: 4, core: 2. Of those that a mesh axis runs over, the one named last changes fastest.
Arguments:
- cells: bfloat16 [16, 4, 64, 32, 128], P('slab', 'lay'), may hold values from -6 to 6
- noise: bfloat16 [16, 4, 64, 128], P('slab', 'lay'), may hold values from -6 to 6
- geometry: bfloat16 [4, 64, 128, 128], P('lay'), may hold values from -0.5 to 0.5
- tile_block: int32 [4, 64], P('lay'), may hold values from 0 to 31
- tile_count: int32 [4], P('lay'), may hold values from 1 to 64, 132 in all
- w_first: bfloat16 [3, 3, 3, 32, 32], replicated, may hold values from -0.21875 to 0.21875
- w_second: bfloat16 [3, 3, 3, 32, 32], replicated, may hold values from -0.21875 to 0.21875
- w_out: bfloat16 [32], replicated, may hold values from -1 to 1
Outputs:
- predicted: bfloat16 [16, 4, 64, 128], P('slab', 'lay')
- grad_first: float32 [3, 3, 3, 32, 32], replicated
- grad_second: float32 [3, 3, 3, 32, 32], replicated
- grad_out: float32 [32], replicated
Inputs may be any that keep to these rules, and one draw needn't show every extreme that they name: `tile_count`: every layer has at least one live tile; the live tiles of all layers number 132, and some layer has exactly 64.
All inputs are finite; a program needn't handle non-finite values. No bound on the sum of `tile_count` on one device may be relied on, other than what follows from the above.
Results may differ from a plain program's by a relative error of at most 0.0095.
Values may be sent and summed in bfloat16 or wider, within the bound.
No kernel may reach another device: no remote copies, remote signals or barrier semaphores. Data moves between devices by JAX's collectives and lax.ppermute only.
A program may use at most 128 MiB of HBM per device.

v0:
```python
import jax
import jax.numpy as jnp
from jax import lax
from jax.sharding import PartitionSpec as P

GR = 64
GP = 64
BLK = 8

F32 = jnp.float32
BF16 = jnp.bfloat16
HIGH = lax.Precision.HIGHEST


def layer_halo(x):
    count = lax.axis_size("lay")
    if count == 1:
        zeros = jnp.zeros_like(x[:, :1])
        return jnp.concatenate([zeros, x, zeros], axis=1)
    below = lax.ppermute(x[:, -1:], "lay", [(i, i + 1) for i in range(count - 1)])
    above = lax.ppermute(x[:, :1], "lay", [(i + 1, i) for i in range(count - 1)])
    return jnp.concatenate([below, x, above], axis=1)


def unfold(x):
    s, d, r, p, c = x.shape
    main = x.reshape(s, d, r, p // BLK, BLK * c)
    left = jnp.roll(main[..., (BLK - 1) * c :], 1, axis=3)
    right = jnp.roll(main[..., :c], -1, axis=3)
    full = jnp.concatenate([left, main, right], axis=-1)
    return jnp.pad(full, ((0, 0), (0, 0), (1, 1), (0, 0), (0, 0)))


def selector():
    shape = (3, BLK + 2, BLK)
    rows_idx = lax.broadcasted_iota(jnp.int32, shape, 1)
    cols_idx = lax.broadcasted_iota(jnp.int32, shape, 2)
    tap_idx = lax.broadcasted_iota(jnp.int32, shape, 0)
    return (rows_idx == cols_idx + tap_idx).astype(F32)


def banded(weight):
    c, o = weight.shape[3], weight.shape[4]
    matrix = jnp.einsum("mqp,ijmco->ijqcpo", selector(), weight.astype(F32), precision=HIGH)
    return matrix.reshape(3, 3, (BLK + 2) * c, BLK * o).astype(BF16)


def band_sum(product, c, o):
    lead = product.shape[:-2]
    product = product.reshape(lead + (BLK + 2, c, BLK, o))
    return jnp.einsum("mqp,...qipo->...mio", selector(), product, precision=HIGH)


def conv_layers(xu, matrices, layers):
    radial = xu.shape[2] - 2
    total = None
    for i in range(3):
        for j in range(3):
            term = jnp.einsum(
                "slrqk,kn->slrqn", xu[:, i : i + layers, j : j + radial], matrices[i, j],
                preferred_element_type=F32,
            )
            total = term if total is None else total + term
    return total


def tree_sum(x, axes):
    for axis in axes:
        size = lax.axis_size(axis)
        if size & (size - 1):
            x = lax.psum(x, axis)
            continue
        step = 1
        while step < size:
            x = x + lax.ppermute(x, axis, [(i, i ^ step) for i in range(size)])
            step *= 2
    return x


def per_device(cells, noise, geometry, tile_block, tile_count, w_first, w_second, w_out):
    showers, layer_count, tile_total, channels, cell_width = cells.shape
    block_total = GR * GP // 128
    slab_count = lax.axis_size("slab")
    lay_count = lax.axis_size("lay")
    nq = GP // BLK
    live_mask = lax.broadcasted_iota(jnp.int32, (layer_count, tile_total), 1) < tile_count[:, None]
    block_ids = lax.broadcasted_iota(jnp.int32, (layer_count, tile_total, block_total), 2)
    onehot = (live_mask[:, :, None] & (tile_block[:, :, None] == block_ids)).astype(F32)
    out_weight = w_out.astype(F32)

    mapped = jnp.einsum("bltcn,ltnp->bltcp", cells, geometry, preferred_element_type=F32)
    grid_sum = jnp.einsum("bltcp,ltk->blkpc", mapped, onehot, precision=HIGH)
    grid = grid_sum.astype(BF16).reshape(showers, layer_count, GR, GP, channels)

    grid_u = unfold(layer_halo(grid))
    first = conv_layers(grid_u, banded(w_first), layer_count)
    first = first.reshape(showers, layer_count, GR, GP, channels)
    active = jax.nn.silu(first).astype(BF16)

    active_u = unfold(active)
    second_band = banded(w_second)
    stacked = jnp.concatenate([second_band[i] for i in range(3)], axis=-1)
    parts = None
    for j in range(3):
        term = jnp.einsum(
            "slrqk,kn->slrqn", active_u[:, :, j : j + GR], stacked[j], preferred_element_type=F32
        )
        parts = term if parts is None else parts + term
    parts = parts.reshape(showers, layer_count, GR, nq, 3, BLK, channels)
    projected = jnp.einsum("blrqitc,c->iblrqt", parts, out_weight, precision=HIGH)
    projected = projected.reshape(3, showers, layer_count, GR, GP)
    lower = layer_halo(projected[0])[:, :layer_count]
    upper = layer_halo(projected[2])[:, 2:]
    grid_f = grid.astype(F32)
    own = jnp.einsum("blrpc,c->blrp", grid_f, out_weight, precision=HIGH)
    pred_grid = (own + projected[1] + lower + upper).astype(BF16)

    block_grid = pred_grid.reshape(showers, layer_count, block_total, 128)
    picked = jnp.einsum(
        "blkp,ltk->bltp", block_grid, onehot.astype(BF16), preferred_element_type=F32
    ).astype(BF16)
    predicted = jnp.einsum(
        "bltp,ltnp->bltn", picked, geometry, preferred_element_type=F32
    ).astype(BF16)
    loss_scale = 32.0 / (showers * slab_count * layer_count * lay_count * GR * GP)
    live_f = live_mask.astype(F32)[None, :, :, None]
    cell_grad = (
        (predicted.astype(F32) - noise.astype(F32)) * live_f * loss_scale
    ).astype(BF16)
    back_map = jnp.einsum("bltn,ltnp->bltp", cell_grad, geometry, preferred_element_type=F32)
    grid_grad = jnp.einsum("bltp,ltk->blkp", back_map, onehot, precision=HIGH)
    grid_grad = grid_grad.astype(BF16).reshape(showers, layer_count, GR, GP)

    grad_h = layer_halo(grid_grad).astype(F32)
    taps_grad = jnp.stack([grad_h[:, 2 - i : 2 - i + layer_count] for i in range(3)], axis=0)
    taps_grad = taps_grad.reshape(3, showers, layer_count, GR, nq, BLK)
    grad_out = jnp.einsum("blrpc,blrp->c", grid_f, grad_h[:, 1 : 1 + layer_count], precision=HIGH)
    grad_out = grad_out + jnp.einsum("blrqitc,iblrqt->c", parts, taps_grad, precision=HIGH)

    second_h = (grad_h[..., None] * out_weight).astype(BF16)
    width = BLK * channels
    taps_second = jnp.concatenate(
        [second_h[:, 2 - i : 2 - i + layer_count].reshape(showers, layer_count, GR, nq, width)
         for i in range(3)],
        axis=-1,
    )
    grad_second = []
    for j in range(3):
        product = jnp.einsum(
            "slrqk,slrqn->kn", active_u[:, :, j : j + GR], taps_second, preferred_element_type=F32
        )
        product = product.reshape(product.shape[0], 3, width)
        grad_second.append(jnp.stack([band_sum(product[:, i], channels, channels) for i in range(3)]))
    grad_second = jnp.stack(grad_second, axis=1)

    flipped = jnp.swapaxes(jnp.flip(w_second, (0, 1, 2)), 3, 4)
    active_grad = conv_layers(unfold(second_h), banded(flipped), layer_count)
    active_grad = active_grad.reshape(showers, layer_count, GR, GP, channels)
    sigmoid_z = jax.nn.sigmoid(first)
    first_grad = (active_grad * sigmoid_z * (1.0 + first * (1.0 - sigmoid_z))).astype(BF16)
    first_grad = first_grad.reshape(showers, layer_count, GR, nq, width)
    grad_first = []
    for i in range(3):
        for j in range(3):
            product = jnp.einsum(
                "slrqk,slrqn->kn", grid_u[:, i : i + layer_count, j : j + GR], first_grad,
                preferred_element_type=F32,
            )
            grad_first.append(band_sum(product, channels, channels))
    grad_first = jnp.stack(grad_first).reshape(3, 3, 3, channels, channels)

    size = grad_first.size
    flat = jnp.concatenate([grad_first.reshape(-1), grad_second.reshape(-1), grad_out])
    flat = tree_sum(flat, ("slab", "lay"))
    grad_first = flat[:size].reshape(grad_first.shape)
    grad_second = flat[size : 2 * size].reshape(grad_first.shape)
    grad_out = flat[2 * size :]
    return (predicted, grad_first, grad_second, grad_out)


def solution(mesh):
    in_specs = (
        P("slab", "lay", None, None, None),
        P("slab", "lay", None, None),
        P("lay", None, None, None),
        P("lay", None),
        P("lay"),
        P(),
        P(),
        P(),
    )
    out_specs = (P("slab", "lay", None, None), P(), P(), P())
    return jax.shard_map(
        per_device, mesh=mesh, in_specs=in_specs, out_specs=out_specs, check_vma=False
    )
```

profile of v0, /device:TPU:28, one launch (start us, length us, event | category | flops | bytes accessed | tf_op | source)
XLA Modules:
  0.0 331.4 jit_solution(17035062872203945451)
XLA Ops:
  7.7 3.3 copy.171
  11.0 3.5 %collective-permute-start.1 = (bf16[2,1,64,64,32]{2,4,3,0,1:T(8,128)(2,1)}, bf16[2,1,64,64,32]{2,4,3,0,1:T(8,128)(2,1)}, u32[]{:S(2)}, u32[]{:S(2)}) collective-permute-start(bf16[2,1,64,64,32]{2,4,3,0,1:T(8,128)(2,1)} %copy.171), channel_id=1, source_target_pairs={{8,0},{16,8},{24,16},{9,1},{17,9},{25,17},{10,2},{18,10},{26,18},{... | collective-permute-start | bytes 1572872 | tf_op jit(solution)/shard_map/ppermute | solution.py:21
  14.4 3.8 %collective-permute-start = (bf16[2,1,64,64,32]{2,4,3,0,1:T(8,128)(2,1)}, bf16[2,1,64,64,32]{2,4,3,0,1:T(8,128)(2,1)}, u32[]{:S(2)}, u32[]{:S(2)}) collective-permute-start(bf16[2,1,64,64,32]{2,4,3,0,1:T(8,128)(2,1)} %copy.171), channel_id=1, source_target_pairs={{0,8},{8,16},{16,24},{1,9},{9,17},{17,25},{2,10},{10,18},{18,26},{... | collective-permute-start | bytes 1572872 | tf_op jit(solution)/shard_map/ppermute | solution.py:20
  21.5 3.2 convert_bitcast_fusion.1
  25.5 3.7 %fusion.301 = (bf16[1,3,10,32,8,32]{5,2,3,1,0,4:T(8,128)(2,1)}, bf16[1,3,10,32,8,32]{5,2,3,1,0,4:T(8,128)(2,1)}, bf16[1,3,10,32,8,32]{5,2,3,1,0,4:T(8,128)(2,1)S(1)}) fusion(bf16[3,3,10,32,8,32]{5,2,3,1,0,4:T(8,128)(2,1)S(1)} %convert_bitcast_fusion.1), kind=kLoop, calls=%fused_computation.318 | loop fusion | bytes 2949120 | tf_op jit(solution)/shard_map/slice | solution.py:102
  34.8 4.4 %copy.180 = bf16[1,3,10,32,8,32]{5,4,3,2,1,0:T(8,128)(2,1)} copy(bf16[1,3,10,32,8,32]{5,2,3,1,0,4:T(8,128)(2,1)} %get-tuple-element.19) | data formatting | bytes 983040 | tf_op jit(solution)/shard_map/slice | solution.py:102
  39.2 3.7 %squeeze.91 = bf16[3,320,256]{2,1,0:T(8,128)(2,1)} reshape(bf16[1,3,10,32,8,32]{5,4,3,2,1,0:T(8,128)(2,1)} %copy.180) | data formatting | bytes 983040 | tf_op jit(solution)/shard_map/squeeze | solution.py:102
  42.9 4.4 %copy.181 = bf16[1,3,10,32,8,32]{5,4,3,2,1,0:T(8,128)(2,1)} copy(bf16[1,3,10,32,8,32]{5,2,3,1,0,4:T(8,128)(2,1)} %get-tuple-element.18) | data formatting | bytes 983040 | tf_op jit(solution)/shard_map/slice | solution.py:102
  47.3 3.7 %squeeze.92 = bf16[3,320,256]{2,1,0:T(8,128)(2,1)} reshape(bf16[1,3,10,32,8,32]{5,4,3,2,1,0:T(8,128)(2,1)} %copy.181) | data formatting | bytes 983040 | tf_op jit(solution)/shard_map/squeeze | solution.py:102
  51.0 3.1 concatenate.59
  54.2 3.7 %convert_bitcast_fusion.2 = bf16[3,3,10,32,8,32]{5,2,3,1,0,4:T(8,128)(2,1)S(1)} fusion(bf16[3,3,3,32,32]{4,3,2,1,0:T(8,128)(2,1)S(1)} %copy-done.27), kind=kOutput, calls=%fused_computation.2 | convolution fusion | flops 5161440 | bytes 1529856 | tf_op jit(solution)/shard_map/mqp,ijmco->ijqcpo/dot_general | solution.py:44
  57.9 6.8 %copy.177 = bf16[3,3,10,32,8,32]{5,4,3,2,1,0:T(8,128)(2,1)} copy(bf16[3,3,10,32,8,32]{5,2,3,1,0,4:T(8,128)(2,1)S(1)} %convert_bitcast_fusion.2) | data formatting | bytes 2949120 | tf_op jit(solution)/shard_map/convert_element_type | solution.py:45
  64.7 8.1 %convert_element_type.204 = bf16[3,3,320,256]{3,2,1,0:T(8,128)(2,1)} reshape(bf16[3,3,10,32,8,32]{5,4,3,2,1,0:T(8,128)(2,1)} %copy.177) | data formatting | bytes 2949120 | tf_op jit(solution)/shard_map/convert_element_type | solution.py:45
  74.0 5.4 %convert_bitcast_fusion = bf16[3,3,10,32,8,32]{5,2,3,1,0,4:T(8,128)(2,1)} fusion(bf16[3,3,3,32,32]{4,2,3,1,0:T(4,128)(2,1)S(1)} %copy.194), kind=kOutput, calls=%fused_computation | convolution fusion | flops 5161440 | bytes 1529856 | tf_op jit(solution)/shard_map/mqp,ijmco->ijqcpo/dot_general | solution.py:44
  80.3 10.4 %copy.195 = bf16[3,3,10,32,8,32]{5,4,3,2,1,0:T(8,128)(2,1)} copy(bf16[3,3,10,32,8,32]{5,2,3,1,0,4:T(8,128)(2,1)} %convert_bitcast_fusion) | data formatting | bytes 2949120 | tf_op jit(solution)/shard_map/convert_element_type | solution.py:45
  90.6 8.2 %convert_element_type.229 = bf16[3,3,320,256]{3,2,1,0:T(8,128)(2,1)} reshape(bf16[3,3,10,32,8,32]{5,4,3,2,1,0:T(8,128)(2,1)} %copy.195) | data formatting | bytes 2949120 | tf_op jit(solution)/shard_map/convert_element_type | solution.py:45
  107.6 4.4 %fusion.3 = bf16[2,3,64,8,320]{4,3,2,0,1:T(8,128)(2,1)S(1)} fusion(bf16[2,1,64,8,256]{4,3,2,0,1:T(8,128)(2,1)S(1)} %copy.175, bf16[2,1,64,8,256]{4,3,2,0,1:T(8,128)(2,1)S(1)} %concatenate.59, bf16[2,1,64,8,256]{4,3,2,0,1:T(8,128)(2,1)S(1)} %copy-done.4, bf16[2,3,64,7,32]{4,3,2,0,1:T(8,128)(2,1)S(1)} %get-tuple-element.38, ...), kind=kLoop, calls=%fused_computation.11 | loop fusion | flops 21626880 | bytes 3883008 | tf_op jit(solution)/shard_map/concatenate | solution.py:30
  119.7 3.4 %fusion.220 = (bf16[320,8,64,2]{0,1,2,3:T(8,128)(2,1)}, bf16[320,8,64,2]{0,1,2,3:T(8,128)(2,1)}, bf16[320,8,64,2]{0,1,2,3:T(8,128)(2,1)}, bf16[320,8,64,2]{0,1,2...) fusion(bf16[2,3,64,8,320]{4,3,2,0,1:T(8,128)(2,1)S(1)} %fusion.3), kind=kLoop, calls=%fused_computation.220 | loop fusion | bytes 10616832 | tf_op jit(solution)/shard_map/slrqk,slrqn->kn/dot_general | solution.py:165
  125.9 5.8 %copy.182 = f32[2,64,8,768]{1,3,2,0:T(8,128)} copy(f32[2,64,8,768]{3,2,1,0:T(8,128)} %add_add_fusion) | data formatting | bytes 6291456 | tf_op jit(solution)/shard_map/add | solution.py:108
  131.7 4.9 %fusion.282 = f32[1,2,64,8,3,8]{2,0,5,4,3,1:T(1,128)S(1)} fusion(f32[2,64,8,3,8,32]{1,5,4,3,2,0:T(8,128)} %bitcast.722, bf16[32]{0:T(256)(128)(2,1)S(1)} %copy-done.36), kind=kOutput, calls=%fused_computation.299 | convolution fusion | flops 9437184 | bytes 3244096 | tf_op jit(solution)/shard_map/blrqitc,c->iblrqt/dot_general | solution.py:110
  136.7 3.2 collective-permute-start.3
  173.8 4.1 %collective-permute-start.5 = (bf16[2,1,64,64]{2,3,0,1:T(8,128)(2,1)S(1)}, bf16[2,1,64,64]{2,3,0,1:T(8,128)(2,1)S(1)}, u32[]{:S(2)}, u32[]{:S(2)}) collective-permute-start(bf16[2,1,64,64]{2,3,0,1:T(8,128)(2,1)S(1)} %copy.189), channel_id=1, source_target_pairs={{8,0},{16,8},{24,16},{9,1},{17,9},{25,17},{10,2},{18,10},{26,18},{... | collective-permute-start | bytes 49160 | tf_op jit(solution)/shard_map/ppermute | solution.py:21
  181.6 3.1 collective-permute-done.4
  185.4 3.1 mul.99
  188.5 6.2 %copy.193 = f32[2,3,64,8,256]{4,3,2,0,1:T(8,128)} copy(f32[2,3,64,8,256]{2,4,3,0,1:T(8,128)} %bitcast.724) | data formatting | bytes 6291456 | tf_op jit(solution)/shard_map/mul | solution.py:140
  202.9 4.4 %copy.235 = bf16[3,256,8,64,2]{1,3,4,2,0:T(8,128)(2,1)} copy(bf16[3,256,8,64,2]{3,1,0,2,4:T(8,128)(2,1)} %bitcast.726) | data formatting | bytes 3145728 | tf_op jit(solution)/shard_map/slrqk,slrqn->kn/dot_general | solution.py:149
  244.9 4.5 %maximum_maximum_fusion = bf16[2,3,64,8,320]{4,3,2,0,1:T(8,128)(2,1)S(1)} fusion(bf16[2,3,64,1,32]{4,3,2,0,1:T(2,128)(2,1)S(1)} %copy-done.26, bf16[2,3,64,7,32]{4,3,2,0,1:T(8,128)(2,1)} %get-tuple-element.36, bf16[2,3,64,8,256]{4,3,2,0,1:T(8,128)(2,1)S(1)} %multiply_convert_fusion.1, bf16[2,3,64,7,32]{4,3,2,0,1:T(8,128)(2,1)S(1)} %copy-done.8, ...), kind=kLoop, calls=%fused_computation.17 | loop fusion | flops 9830400 | bytes 3932160 | tf_op jit(solution)/shard_map/concatenate | solution.py:30
  285.9 7.0 %fusion.161 = f32[32]{0:T(128)S(1)} fusion(f32[32]{0:T(128)S(1)} %multiply_reduce_fusion, f32[2,64,8,3,8,32]{1,5,4,3,2,0:T(8,128)} %bitcast.723, f32[3,2,64,8,8,1]{2,4,3,1,0,5:T(8,128)S(1)} %maximum_bitcast_fusion.3), kind=kOutput, calls=%fused_computation.153 | convolution fusion | flops 9437216 | bytes 3244288 | tf_op jit(solution)/shard_map/blrqitc,iblrqt->c/dot_general | solution.py:138
  295.0 7.1 %collective-permute-done.7 = f32[55328]{0:T(1024)S(1)} collective-permute-done((f32[55328]{0:T(1024)S(1)}, f32[55328]{0:T(1024)S(1)}, u32[]{:S(2)}, u32[]{:S(2)}) %collective-permute-start.7) | collective-permute-done | bytes 221344 | tf_op jit(solution)/shard_map/ppermute | solution.py:75
  302.6 12.0 %collective-permute-done.8 = f32[55328]{0:T(1024)S(1)} collective-permute-done((f32[55328]{0:T(1024)S(1)}, f32[55328]{0:T(1024)S(1)}, u32[]{:S(2)}, u32[]{:S(2)}) %collective-permute-start.8) | collective-permute-done | bytes 221344 | tf_op jit(solution)/shard_map/ppermute | solution.py:75
  314.7 7.4 %collective-permute-done.9 = f32[55328]{0:T(1024)S(1)} collective-permute-done((f32[55328]{0:T(1024)S(1)}, f32[55328]{0:T(1024)S(1)}, u32[]{:S(2)}, u32[]{:S(2)}) %collective-permute-start.9) | collective-permute-done | bytes 221344 | tf_op jit(solution)/shard_map/ppermute | solution.py:75
  322.2 6.6 %collective-permute-done.10 = f32[55328]{0:T(1024)S(1)} collective-permute-done((f32[55328]{0:T(1024)S(1)}, f32[55328]{0:T(1024)S(1)}, u32[]{:S(2)}, u32[]{:S(2)}) %collective-permute-start.10) | collective-permute-done | bytes 221344 | tf_op jit(solution)/shard_map/ppermute | solution.py:75
  (229 shorter events, 161.8 us)
Async XLA Ops:
  0.6 1.6 copy-start
  2.2 1.9 copy-start.35
  11.0 10.6 %copy-start.23 = (bf16[3,3,3,32,32]{4,3,2,1,0:T(8,128)(2,1)S(1)}, bf16[3,3,3,32,32]{4,3,2,1,0:T(8,128)(2,1)}, u32[]{:S(2)}) copy-start(bf16[3,3,3,32,32]{4,3,2,1,0:T(8,128)(2,1)} %param.14) | copy-start | bytes 165892
  11.0 89.1 %collective-permute-start.1 = (bf16[2,1,64,64,32]{2,4,3,0,1:T(8,128)(2,1)}, bf16[2,1,64,64,32]{2,4,3,0,1:T(8,128)(2,1)}, u32[]{:S(2)}, u32[]{:S(2)}) collective-permute-start(bf16[2,1,64,64,32]{2,4,3,0,1:T(8,128)(2,1)} %copy.171), channel_id=1, source_target_pairs={{8,0},{16,8},{24,16},{9,1},{17,9},{25,17},{10,2},{18,10},{26,18},{... | collective-permute-start | bytes 1572872 | tf_op jit(solution)/shard_map/ppermute | solution.py:21
  14.4 88.5 %collective-permute-start = (bf16[2,1,64,64,32]{2,4,3,0,1:T(8,128)(2,1)}, bf16[2,1,64,64,32]{2,4,3,0,1:T(8,128)(2,1)}, u32[]{:S(2)}, u32[]{:S(2)}) collective-permute-start(bf16[2,1,64,64,32]{2,4,3,0,1:T(8,128)(2,1)} %copy.171), channel_id=1, source_target_pairs={{0,8},{8,16},{16,24},{1,9},{9,17},{17,25},{2,10},{10,18},{18,26},{... | collective-permute-start | bytes 1572872 | tf_op jit(solution)/shard_map/ppermute | solution.py:20
  47.3 6.9 %copy-start.27 = (bf16[3,3,3,32,32]{4,3,2,1,0:T(8,128)(2,1)S(1)}, bf16[3,3,3,32,32]{4,3,2,1,0:T(8,128)(2,1)}, u32[]{:S(2)}) copy-start(bf16[3,3,3,32,32]{4,3,2,1,0:T(8,128)(2,1)} %param.13) | copy-start | bytes 165892
  64.7 8.1 %copy-start.36 = (bf16[32]{0:T(256)(128)(2,1)S(1)}, bf16[32]{0:T(256)(128)(2,1)}, u32[]{:S(2)}) copy-start(bf16[32]{0:T(256)(128)(2,1)} %param.15) | copy-start | bytes 196
  74.0 5.5 %copy-start.5 = (bf16[2,64,64,32]{2,1,3,0:T(8,128)(2,1)S(1)}, bf16[2,64,64,32]{2,1,3,0:T(8,128)(2,1)}, u32[]{:S(2)}) copy-start(bf16[2,64,64,32]{2,1,3,0:T(8,128)(2,1)} %reshape.512) | copy-start | bytes 1572868
  107.6 4.5 %copy-start.2 = (bf16[3,3,320,256]{3,2,1,0:T(8,128)(2,1)S(1)}, bf16[3,3,320,256]{3,2,1,0:T(8,128)(2,1)}, u32[]{:S(2)}) copy-start(bf16[3,3,320,256]{3,2,1,0:T(8,128)(2,1)} %convert_element_type.204) | copy-start | bytes 4423684
  116.0 1.8 copy-start.10
  136.7 33.8 %collective-permute-start.3 = (f32[2,1,64,64]{2,3,0,1:T(8,128)S(1)}, f32[2,1,64,64]{2,3,0,1:T(8,128)S(1)}, u32[]{:S(2)}, u32[]{:S(2)}) collective-permute-start(f32[2,1,64,64]{2,3,0,1:T(8,128)S(1)} %get-tuple-element.60), channel_id=1, source_target_pairs={{8,0},{16,8},{24,16},{9,1},{17,9},{25,17},{10,2},{18,10},{26,18},{... | collective-permute-start | bytes 98312 | tf_op jit(solution)/shard_map/ppermute | solution.py:21
  139.9 30.5 %collective-permute-start.2 = (f32[2,1,64,64]{2,3,0,1:T(8,128)S(1)}, f32[2,1,64,64]{2,3,0,1:T(8,128)S(1)}, u32[]{:S(2)}, u32[]{:S(2)}) collective-permute-start(f32[2,1,64,64]{2,3,0,1:T(8,128)S(1)} %get-tuple-element.59), channel_id=1, source_target_pairs={{0,8},{8,16},{16,24},{1,9},{9,17},{17,25},{2,10},{10,18},{18,26},{... | collective-permute-start | bytes 98312 | tf_op jit(solution)/shard_map/ppermute | solution.py:20
  167.5 4.6 %copy-start.34 = (bf16[2,1,64,128]{3,2,1,0:T(8,128)(2,1)S(1)}, bf16[2,1,64,128]{3,2,1,0:T(8,128)(2,1)}, u32[]{:S(2)}) copy-start(bf16[2,1,64,128]{3,2,1,0:T(8,128)(2,1)} %param.9) | copy-start | bytes 98308
  173.8 7.7 %collective-permute-start.5 = (bf16[2,1,64,64]{2,3,0,1:T(8,128)(2,1)S(1)}, bf16[2,1,64,64]{2,3,0,1:T(8,128)(2,1)S(1)}, u32[]{:S(2)}, u32[]{:S(2)}) collective-permute-start(bf16[2,1,64,64]{2,3,0,1:T(8,128)(2,1)S(1)} %copy.189), channel_id=1, source_target_pairs={{8,0},{16,8},{24,16},{9,1},{17,9},{25,17},{10,2},{18,10},{26,18},{... | collective-permute-start | bytes 49160 | tf_op jit(solution)/shard_map/ppermute | solution.py:21
  178.0 6.7 %collective-permute-start.4 = (bf16[2,1,64,64]{2,3,0,1:T(8,128)(2,1)S(1)}, bf16[2,1,64,64]{2,3,0,1:T(8,128)(2,1)S(1)}, u32[]{:S(2)}, u32[]{:S(2)}) collective-permute-start(bf16[2,1,64,64]{2,3,0,1:T(8,128)(2,1)S(1)} %copy.189), channel_id=1, source_target_pairs={{0,8},{8,16},{16,24},{1,9},{9,17},{17,25},{2,10},{10,18},{18,26},{... | collective-permute-start | bytes 49160 | tf_op jit(solution)/shard_map/ppermute | solution.py:20
  219.6 2.9 copy-start.12
  230.0 2.1 copy-start.13
  242.2 1.7 copy-start.29
  242.2 1.7 copy-start.30
  244.9 4.5 %copy-start.3 = (bf16[3,3,320,256]{3,2,1,0:T(8,128)(2,1)S(1)}, bf16[3,3,320,256]{3,2,1,0:T(8,128)(2,1)}, u32[]{:S(2)}) copy-start(bf16[3,3,320,256]{3,2,1,0:T(8,128)(2,1)} %convert_element_type.229) | copy-start | bytes 4423684
  253.7 2.7 copy-start.22
  256.4 4.4 %copy-start.24 = (bf16[256,8,64,2]{2,1,3,0:T(8,128)(2,1)S(1)}, bf16[256,8,64,2]{2,1,3,0:T(8,128)(2,1)}, u32[]{:S(2)}) copy-start(bf16[256,8,64,2]{2,1,3,0:T(8,128)(2,1)} %copy.196) | copy-start | bytes 1572868
  263.8 1.7 copy-start.17
  284.1 1.7 copy-start.31
  284.1 1.7 copy-start.32
  284.1 1.7 copy-start.33
  292.9 1.5 collective-permute-start.6
  294.5 36.7 %copy-start.1 = (bf16[1,64,128,128]{3,2,1,0:T(8,128)(2,1)S(1)}, bf16[1,64,128,128]{3,2,1,0:T(8,128)(2,1)}, u32[]{:S(2)}) copy-start(bf16[1,64,128,128]{3,2,1,0:T(8,128)(2,1)} %param.10) | copy-start | bytes 6291460
  294.5 7.6 %collective-permute-start.7 = (f32[55328]{0:T(1024)S(1)}, f32[55328]{0:T(1024)S(1)}, u32[]{:S(2)}, u32[]{:S(2)}) collective-permute-start(f32[55328]{0:T(1024)S(1)} %fusion.299), channel_id=1, source_target_pairs={{0,2},{1,3},{2,0},{3,1},{4,6},{5,7},{6,4},{7,5},{8,10},{9,11},{10,... | collective-permute-start | bytes 663944 | tf_op jit(solution)/shard_map/ppermute | solution.py:75
  302.2 12.4 %collective-permute-start.8 = (f32[55328]{0:T(1024)S(1)}, f32[55328]{0:T(1024)S(1)}, u32[]{:S(2)}, u32[]{:S(2)}) collective-permute-start(f32[55328]{0:T(1024)S(1)} %add.280), channel_id=1, source_target_pairs={{0,4},{1,5},{2,6},{3,7},{4,0},{5,1},{6,2},{7,3},{8,12},{9,13},{10,... | collective-permute-start | bytes 663944 | tf_op jit(solution)/shard_map/ppermute | solution.py:75
  314.6 7.5 %collective-permute-start.9 = (f32[55328]{0:T(1024)S(1)}, f32[55328]{0:T(1024)S(1)}, u32[]{:S(2)}, u32[]{:S(2)}) collective-permute-start(f32[55328]{0:T(1024)S(1)} %add.281), channel_id=1, source_target_pairs={{0,8},{8,0},{16,24},{24,16},{1,9},{9,1},{17,25},{25,17},{2,10},{10... | collective-permute-start | bytes 663944 | tf_op jit(solution)/shard_map/ppermute | solution.py:75
  322.1 6.6 %collective-permute-start.10 = (f32[55328]{0:T(1024)S(1)}, f32[55328]{0:T(1024)S(1)}, u32[]{:S(2)}, u32[]{:S(2)}) collective-permute-start(f32[55328]{0:T(1024)S(1)} %add.282), channel_id=1, source_target_pairs={{0,16},{8,24},{16,0},{24,8},{1,17},{9,25},{17,1},{25,9},{2,18},{10... | collective-permute-start | bytes 663944 | tf_op jit(solution)/shard_map/ppermute | solution.py:75
  (16 other events, 21.5 us)
where the time goes:
time: 337 us; the launch traced here: 331 us
  local copies, waits for them, and re-layouts  155 us (46%)
  matrix products  97 us (29%)
  waiting for transfers between devices  37.7 us (11%)
  starting transfers between devices  20.2 us (6%)
  other arithmetic  19 us (6%)
    ppermute x5, waiting for transfers between devices, tree_sum(): x = x + lax.ppermute(x, axis, [(i, i ^ step) for i in range(size)])  34.5 us
    convert_element_type x4, local copies, waits for them, and re-layouts, banded(): return matrix.reshape(3, 3, (BLK + 2) * c, BLK * o).astype(BF16)  33.5 us
    dot_general x18, matrix products, band_sum(): jnp.einsum('mqp,...qipo->...mio', selector(), product, precision=HIGH)  33 us
    dot_general x10, local copies, waits for them, and re-layouts, per_device(): jnp.einsum('slrqk,slrqn->kn', grid_u[:, i:i + layer_count, j:j + GR], fir...  30.1 us
    dot_general x9, matrix products, per_device(): jnp.einsum('slrqk,slrqn->kn', grid_u[:, i:i + layer_count, j:j + GR], fir...  15.3 us
    slice x4, local copies, waits for them, and re-layouts, per_device(): stacked = jnp.concatenate([second_band[i] for i in range(3)], axis=-1)  15.1 us
    dot_general x3, matrix products, banded(): jnp.einsum('mqp,ijmco->ijqcpo', selector(), weight.astype(F32), precision...  12.4 us
    ppermute x3, starting transfers between devices, layer_halo(): lax.ppermute(x[:, :1], 'lay', [(i + 1, i) for i in range(count - 1)])  10.8 us
  transfers between devices with their start and end apart: 11, of which 6 were waited for; matrix products, arithmetic and copies ran while one was open for 34% of the time, Pallas kernels for 0%

commit v1 on v0

--- a/solution.py
+++ b/solution.py
@@ -41,27 +41,21 @@
 
 def banded(weight):
     c, o = weight.shape[3], weight.shape[4]
-    matrix = jnp.einsum("mqp,ijmco->ijqcpo", selector(), weight.astype(F32), precision=HIGH)
-    return matrix.reshape(3, 3, (BLK + 2) * c, BLK * o).astype(BF16)
+    rows, cols = (BLK + 2) * c, BLK * o
+    tap = (lax.broadcasted_iota(jnp.int32, (rows, cols), 0) // c
+           - lax.broadcasted_iota(jnp.int32, (rows, cols), 1) // o)
+    tiled = jnp.tile(weight, (1, 1, 1, BLK + 2, BLK))
+    out = jnp.zeros((3, 3, rows, cols), weight.dtype)
+    for m in range(3):
+        out = jnp.where((tap == m)[None, None], tiled[:, :, m], out)
+    return out
 
 
-def band_sum(product, c, o):
-    lead = product.shape[:-2]
-    product = product.reshape(lead + (BLK + 2, c, BLK, o))
-    return jnp.einsum("mqp,...qipo->...mio", selector(), product, precision=HIGH)
-
-
-def conv_layers(xu, matrices, layers):
+def columns(xu, layers, layer_taps):
     radial = xu.shape[2] - 2
-    total = None
-    for i in range(3):
-        for j in range(3):
-            term = jnp.einsum(
-                "slrqk,kn->slrqn", xu[:, i : i + layers, j : j + radial], matrices[i, j],
-                preferred_element_type=F32,
-            )
-            total = term if total is None else total + term
-    return total
+    pieces = [xu[:, i : i + layers, j : j + radial] for i in range(layer_taps) for j in range(3)]
+    x = jnp.concatenate(pieces, axis=-1)
+    return x.reshape(-1, x.shape[-1])
 
 
 def tree_sum(x, axes):
@@ -92,23 +86,23 @@
     grid_sum = jnp.einsum("bltcp,ltk->blkpc", mapped, onehot, precision=HIGH)
     grid = grid_sum.astype(BF16).reshape(showers, layer_count, GR, GP, channels)
 
-    grid_u = unfold(layer_halo(grid))
-    first = conv_layers(grid_u, banded(w_first), layer_count)
+    rows = showers * layer_count * GR * nq
+    width = BLK * channels
+    grid_x = columns(unfold(layer_halo(grid)), layer_count, 3)
+    first = jnp.dot(grid_x, banded(w_first).reshape(-1, width), preferred_element_type=F32)
     first = first.reshape(showers, layer_count, GR, GP, channels)
     active = jax.nn.silu(first).astype(BF16)
 
-    active_u = unfold(active)
-    second_band = banded(w_second)
-    stacked = jnp.concatenate([second_band[i] for i in range(3)], axis=-1)
-    parts = None
-    for j in range(3):
-        term = jnp.einsum(
-            "slrqk,kn->slrqn", active_u[:, :, j : j + GR], stacked[j], preferred_element_type=F32
-        )
-        parts = term if parts is None else parts + term
-    parts = parts.reshape(showers, layer_count, GR, nq, 3, BLK, channels)
-    projected = jnp.einsum("blrqitc,c->iblrqt", parts, out_weight, precision=HIGH)
-    projected = projected.reshape(3, showers, layer_count, GR, GP)
+    active_x = columns(unfold(active), layer_count, 1)
+    second_band = jnp.transpose(banded(w_second), (1, 2, 0, 3))
+    second_band = second_band.reshape(3 * second_band.shape[1], 3 * width)
+    parts = jnp.dot(active_x, second_band, preferred_element_type=F32)
+    lane = lax.broadcasted_iota(jnp.int32, (3 * width, 3 * BLK), 0)
+    slot = lax.broadcasted_iota(jnp.int32, (3 * width, 3 * BLK), 1)
+    project = jnp.where(lane // channels == slot, jnp.tile(out_weight, 3 * BLK)[:, None], 0.0)
+    projected = jnp.dot(parts, project, precision=HIGH)
+    projected = projected.reshape(showers, layer_count, GR, nq, 3, BLK)
+    projected = jnp.transpose(projected, (4, 0, 1, 2, 3, 5)).reshape(3, showers, layer_count, GR, GP)
     lower = layer_halo(projected[0])[:, :layer_count]
     upper = layer_halo(projected[2])[:, 2:]
     grid_f = grid.astype(F32)
@@ -132,42 +126,35 @@
     grid_grad = grid_grad.astype(BF16).reshape(showers, layer_count, GR, GP)
 
     grad_h = layer_halo(grid_grad).astype(F32)
-    taps_grad = jnp.stack([grad_h[:, 2 - i : 2 - i + layer_count] for i in range(3)], axis=0)
-    taps_grad = taps_grad.reshape(3, showers, layer_count, GR, nq, BLK)
+    taps_grad = jnp.stack(
+        [grad_h[:, 2 - i : 2 - i + layer_count].reshape(showers, layer_count, GR, nq, BLK)
+         for i in range(3)],
+        axis=4,
+    ).reshape(rows, 3 * BLK)
     grad_out = jnp.einsum("blrpc,blrp->c", grid_f, grad_h[:, 1 : 1 + layer_count], precision=HIGH)
-    grad_out = grad_out + jnp.einsum("blrqitc,iblrqt->c", parts, taps_grad, precision=HIGH)
+    weighted = parts.reshape(rows, 3 * BLK, channels) * taps_grad[:, :, None]
+    grad_out = grad_out + jnp.sum(weighted, axis=(0, 1))
 
     second_h = (grad_h[..., None] * out_weight).astype(BF16)
-    width = BLK * channels
     taps_second = jnp.concatenate(
-        [second_h[:, 2 - i : 2 - i + layer_count].reshape(showers, layer_count, GR, nq, width)
-         for i in range(3)],
-        axis=-1,
+        [second_h[:, 2 - i : 2 - i + layer_count].reshape(rows, width) for i in range(3)], axis=-1
     )
-    grad_second = []
-    for j in range(3):
-        product = jnp.einsum(
-            "slrqk,slrqn->kn", active_u[:, :, j : j + GR], taps_second, preferred_element_type=F32
-        )
-        product = product.reshape(product.shape[0], 3, width)
-        grad_second.append(jnp.stack([band_sum(product[:, i], channels, channels) for i in range(3)]))
-    grad_second = jnp.stack(grad_second, axis=1)
+    product = lax.dot_general(
+        taps_second, active_x, (((0,), (0,)), ((), ())), preferred_element_type=F32
+    ).reshape(3, BLK, channels, 3, BLK + 2, channels)
+    grad_second = jnp.einsum("mqp,ipojqc->ijmco", selector(), product, precision=HIGH)
 
     flipped = jnp.swapaxes(jnp.flip(w_second, (0, 1, 2)), 3, 4)
-    active_grad = conv_layers(unfold(second_h), banded(flipped), layer_count)
+    second_x = columns(unfold(second_h), layer_count, 3)
+    active_grad = jnp.dot(second_x, banded(flipped).reshape(-1, width), preferred_element_type=F32)
     active_grad = active_grad.reshape(showers, layer_count, GR, GP, channels)
     sigmoid_z = jax.nn.sigmoid(first)
     first_grad = (active_grad * sigmoid_z * (1.0 + first * (1.0 - sigmoid_z))).astype(BF16)
-    first_grad = first_grad.reshape(showers, layer_count, GR, nq, width)
-    grad_first = []
-    for i in range(3):
-        for j in range(3):
-            product = jnp.einsum(
-                "slrqk,slrqn->kn", grid_u[:, i : i + layer_count, j : j + GR], first_grad,
-                preferred_element_type=F32,
-            )
-            grad_first.append(band_sum(product, channels, channels))
-    grad_first = jnp.stack(grad_first).reshape(3, 3, 3, channels, channels)
+    product = lax.dot_general(
+        first_grad.reshape(rows, width), grid_x, (((0,), (0,)), ((), ())),
+        preferred_element_type=F32,
+    ).reshape(BLK, channels, 3, 3, BLK + 2, channels)
+    grad_first = jnp.einsum("mqp,poijqc->ijmco", selector(), product, precision=HIGH)
 
     size = grad_first.size
     flat = jnp.concatenate([grad_first.reshape(-1), grad_second.reshape(-1), grad_out])

time: 337 us -> 393 us (1.17)
  local copies, waits for them, and re-layouts: 155 us -> 218 us
  matrix products: 97 us -> 75.8 us
  other arithmetic: 19 us -> 30.4 us
    another operation x17 -> x12, local copies, waits for them, and re-layouts: 13.8 us -> 85.6 us  [the longest x6 83.5 us: banded(): tiled = jnp.tile(weight, (1, 1, 1, BLK + 2, BLK))]
    concatenate x1 -> x5, local copies, waits for them, and re-layouts: 0.03 us -> 36.4 us  [columns(): x = jnp.concatenate(pieces, axis=-1)]
    convert_element_type x5 -> x2, local copies, waits for them, and re-layouts: 35.7 us -> 1.35 us  [the longest x1 1.24 us: per_device(): active = jax.nn.silu(first).astype(BF16)]
    unnamed x76 -> x48, local copies, waits for them, and re-layouts: 5.57 us -> 28.7 us
    dot_general x56 -> x8, matrix products: 90.2 us -> 69.1 us  [the longest x1 18.2 us: per_device(): jnp.einsum('mqp,poijqc->ijmco', selector(), product, precision=HIGH)]
    dot_general x12 -> x4, local copies, waits for them, and re-layouts: 34.5 us -> 15.6 us  [the longest x1 8.39 us: per_device(): lax.dot_general(first_grad.reshape(rows, width), grid_x, (((0,), (0,)), (...]
    reshape x0 -> x5, local copies, waits for them, and re-layouts: none -> 10.6 us  [the longest x3 8.39 us: per_device(): second_h[:, 2 - i:2 - i + layer_count].reshape(rows, width)]
    squeeze x4 -> x0, local copies, waits for them, and re-layouts: 10.4 us -> none  [the longest x3 10.4 us: per_device(): stacked = jnp.concatenate([second_band[i] for i in range(3)], axis=-1)]
  transfers between devices with their start and end apart: 11 -> 11, of which waited for: 6 -> 6; matrix products, arithmetic and copies ran while one was open for 34% -> 31% of each run, Pallas kernels for 0% -> 0%
where the time goes in v1:
time: 393 us; the launch traced here: 386 us
  local copies, waits for them, and re-layouts  218 us (55%)
  matrix products  75.8 us (19%)
  waiting for transfers between devices  38.9 us (10%)
  other arithmetic  30.4 us (8%)
  starting transfers between devices  20.4 us (5%)
    another operation x6, local copies, waits for them, and re-layouts, banded(): tiled = jnp.tile(weight, (1, 1, 1, BLK + 2, BLK))  83.5 us
    concatenate x5, local copies, waits for them, and re-layouts, columns(): x = jnp.concatenate(pieces, axis=-1)  36.4 us
    ppermute x5, waiting for transfers between devices, tree_sum(): x = x + lax.ppermute(x, axis, [(i, i ^ step) for i in range(size)])  34.5 us
    unnamed x48, local copies, waits for them, and re-layouts  28.7 us
    dot_general x1, matrix products, per_device(): jnp.einsum('mqp,poijqc->ijmco', selector(), product, precision=HIGH)  18.2 us
    dot_general x1, matrix products, per_device(): jnp.einsum('mqp,ipojqc->ijmco', selector(), product, precision=HIGH)  16.4 us
    ppermute x3, starting transfers between devices, layer_halo(): lax.ppermute(x[:, :1], 'lay', [(i + 1, i) for i in range(count - 1)])  10.8 us
    concatenate x3, other arithmetic, unfold(): full = jnp.concatenate([left, main, right], axis=-1)  8.8 us
  transfers between devices with their start and end apart: 11, of which 6 were waited for; matrix products, arithmetic and copies ran while one was open for 31% of the time, Pallas kernels for 0%

profile of v1, /device:TPU:28, one launch (start us, length us, event | category | flops | bytes accessed | tf_op | source)
XLA Modules:
  0.0 385.8 jit_solution(4882446628072536981)
XLA Ops:
  10.9 3.3 collective-permute-start.1
  14.2 4.0 %collective-permute-start = (bf16[2,1,64,64,32]{2,4,3,0,1:T(8,128)(2,1)}, bf16[2,1,64,64,32]{2,4,3,0,1:T(8,128)(2,1)}, u32[]{:S(2)}, u32[]{:S(2)}) collective-permute-start(bf16[2,1,64,64,32]{2,4,3,0,1:T(8,128)(2,1)} %copy.137), channel_id=1, source_target_pairs={{0,8},{8,16},{16,24},{1,9},{9,17},{17,25},{2,10},{10,18},{18,26},{... | collective-permute-start | bytes 1572872 | tf_op jit(solution)/shard_map/ppermute | solution.py:20
  18.5 6.4 %tile.38 = bf16[3,3,3,10,32,8,32]{6,5,4,3,2,1,0:T(8,128)(2,1)} broadcast(bf16[3,3,3,32,32]{4,3,2,1,0:T(8,128)(2,1)S(1)} %copy.156), dimensions={0,1,2,4,6} | broadcast | bytes 4478976 | tf_op jit(solution)/shard_map/tile | solution.py:47
  24.9 21.5 %tile.39 = bf16[3,3,3,320,256]{4,3,2,1,0:T(8,128)(2,1)} reshape(bf16[3,3,3,10,32,8,32]{6,5,4,3,2,1,0:T(8,128)(2,1)} %tile.38) | data formatting | bytes 8847360 | tf_op jit(solution)/shard_map/tile | solution.py:47
  46.3 6.4 %tile.16 = bf16[3,3,3,10,32,8,32]{6,5,4,3,2,1,0:T(8,128)(2,1)} broadcast(bf16[3,3,3,32,32]{4,3,2,1,0:T(8,128)(2,1)S(1)} %copy-done.9), dimensions={0,1,2,4,6} | broadcast | bytes 4478976 | tf_op jit(solution)/shard_map/tile | solution.py:47
  52.7 21.5 %tile.17 = bf16[3,3,3,320,256]{4,3,2,1,0:T(8,128)(2,1)} reshape(bf16[3,3,3,10,32,8,32]{6,5,4,3,2,1,0:T(8,128)(2,1)} %tile.16) | data formatting | bytes 8847360 | tf_op jit(solution)/shard_map/tile | solution.py:47
  74.2 6.4 %tile.14 = bf16[3,3,3,10,32,8,32]{6,5,4,3,2,1,0:T(8,128)(2,1)} broadcast(bf16[3,3,3,32,32]{4,3,2,1,0:T(8,128)(2,1)S(1)} %copy-done.10), dimensions={0,1,2,4,6} | broadcast | bytes 4478976 | tf_op jit(solution)/shard_map/tile | solution.py:47
  80.6 21.4 %tile.15 = bf16[3,3,3,320,256]{4,3,2,1,0:T(8,128)(2,1)} reshape(bf16[3,3,3,10,32,8,32]{6,5,4,3,2,1,0:T(8,128)(2,1)} %tile.14) | data formatting | bytes 8847360 | tf_op jit(solution)/shard_map/tile | solution.py:47
  102.2 7.6 %fusion.23 = (bf16[3,3,320,256]{3,2,1,0:T(8,128)(2,1)}, bf16[3,320,3,256]{3,1,0,2:T(8,128)(2,1)}, bf16[3,3,320,256]{3,2,1,0:T(8,128)(2,1)}) fusion(bf16[3,3,3,320,256]{4,3,2,1,0:T(8,128)(2,1)} %tile.39, pred[320,256]{1,0:T(8,128)(4,1)S(1)} %get-tuple-element.48, pred[320,256]{1,0:T(8,128)(4,1)S(1)} %get-tuple-element.47, ...), kind=kLoop, calls=%fused_computation.50 | loop fusion | flops 6635520 | bytes 17940480 | tf_op jit(solution)/shard_map/jit(_where)/select_n | solution.py:50
  113.1 3.8 concatenate.74
  122.7 5.5 %fusion.6 = bf16[2,3,64,8,320]{2,4,3,0,1:T(8,128)(2,1)S(1)} fusion(bf16[2,1,64,8,256]{2,4,3,0,1:T(8,128)(2,1)} %bitcast.23, bf16[2,1,64,8,256]{2,4,3,0,1:T(8,128)(2,1)S(1)} %copy.140, bf16[2,1,64,8,256]{2,4,3,0,1:T(8,128)(2,1)} %bitcast.22), kind=kLoop, calls=%fused_computation.9 | loop fusion | flops 29491200 | bytes 3538944 | tf_op jit(solution)/shard_map/concatenate | solution.py:30
  141.6 14.2 %copy.141 = bf16[2,1,64,8,2880]{4,3,2,0,1:T(8,128)(2,1)} copy(bf16[2,1,64,8,2880]{2,4,3,0,1:T(8,128)(2,1)} %fusion.37) | data formatting | bytes 11796480 | tf_op jit(solution)/shard_map/concatenate | solution.py:57
  155.8 6.2 %multiply_convert_fusion.1 = (bf16[1024,256]{0,1:T(8,128)(2,1)}, f32[1024,256]{0,1:T(8,128)}) fusion(bf16[1024,2880]{1,0:T(8,128)(2,1)} %bitcast.313, bf16[2880,256]{1,0:T(8,128)(2,1)} %bitcast.328), kind=kOutput, calls=%fused_computation.105 | convolution fusion | flops 1511260160 | bytes 8945664 | tf_op jit(solution)/shard_map/dot_general | solution.py:92
  169.0 4.8 %concatenate.88 = bf16[1024,960]{1,0:T(8,128)(2,1)} concatenate(bf16[1024,320]{1,0:T(8,128)(2,1)} %bitcast.323, bf16[1024,32]{1,0:T(8,128)(2,1)} %bitcast.329, bf16[1024,256]{1,0:T(8,128)(2,1)S(1)} %copy.145, bf16[1024,32]{1,0:T(8,128)(2,1)} %bitcast.330, bf16[1024,320]{1,0:T(8,128)(2,1)S(1)} %bitcast.322), dimensions={1} | concatenate | bytes 3932160 | tf_op jit(solution)/shard_map/concatenate | solution.py:57
  173.8 3.8 fusion.125
  197.8 4.0 %copy.172 = bf16[960,1024]{1,0:T(8,128)(2,1)} copy(bf16[960,1024]{0,1:T(8,128)(2,1)} %bitcast.316) | data formatting | bytes 3932160 | tf_op jit(solution)/shard_map/dot_general | solution.py:142
  201.8 8.4 %copy.168 = bf16[2880,1024]{1,0:T(8,128)(2,1)} copy(bf16[2880,1024]{0,1:T(8,128)(2,1)} %bitcast.314) | data formatting | bytes 11796480 | tf_op jit(solution)/shard_map/dot_general | solution.py:153
  214.3 4.2 %collective-permute-start.5 = (bf16[2,1,64,64]{2,3,0,1:T(8,128)(2,1)S(1)}, bf16[2,1,64,64]{2,3,0,1:T(8,128)(2,1)S(1)}, u32[]{:S(2)}, u32[]{:S(2)}) collective-permute-start(bf16[2,1,64,64]{2,3,0,1:T(8,128)(2,1)S(1)} %copy.162), channel_id=1, source_target_pairs={{8,0},{16,8},{24,16},{9,1},{17,9},{25,17},{10,2},{18,10},{26,18},{... | collective-permute-start | bytes 49160 | tf_op jit(solution)/shard_map/ppermute | solution.py:21
  220.8 4.3 %collective-permute-done.4 = bf16[2,1,64,64]{2,3,0,1:T(8,128)(2,1)S(1)} collective-permute-done((bf16[2,1,64,64]{2,3,0,1:T(8,128)(2,1)S(1)}, bf16[2,1,64,64]{2,3,0,1:T(8,128)(2,1)S(1)}, u32[]{:S(2)}, u32[]{:S(2)}) %collective-permute-start.4) | collective-permute-done | bytes 16416 | tf_op jit(solution)/shard_map/ppermute | solution.py:20
  232.6 3.8 copy.176
  239.6 3.9 multiply_convert_fusion
  243.5 4.7 %fusion.117 = (bf16[2,1,64,64,32]{4,3,2,0,1:T(8,128)(2,1)S(1)}, bf16[2,1,64,64,32]{4,3,2,0,1:T(8,128)(2,1)}, bf16[2,1,64,64,32]{4,3,2,0,1:T(8,128)(2,1)}) fusion(bf16[2,3,64,64,32]{4,3,2,0,1:T(8,128)(2,1)S(1)} %multiply_convert_fusion), kind=kLoop, calls=%fused_computation.184 | loop fusion | bytes 3145728 | tf_op jit(solution)/shard_map/slice | solution.py:140
  259.3 8.3 %fusion.127 = f32[3,8,32,3,10,32]{5,2,4,3,1,0:T(8,128)S(1)} fusion(bf16[3,8,32,1024,1,1]{3,2,5,4,1,0:T(8,128)(2,1)} %bitcast.325, bf16[3,10,32,1024,1,1]{3,2,1,0,5,4:T(8,128)(2,1)} %bitcast.324), kind=kOutput, calls=%fused_computation.194 | convolution fusion | flops 1509949440 | bytes 6488064 | tf_op jit(solution)/shard_map/dot_general | solution.py:142
  267.6 16.4 %fusion.51 = f32[3,3,3,32,32]{3,2,1,4,0:T(4,128)S(1)} fusion(f32[3,8,32,3,10,32]{5,2,4,3,1,0:T(8,128)S(1)} %fusion.127), kind=kOutput, calls=%fused_computation.89 | convolution fusion | flops 26542560 | bytes 3059712 | tf_op jit(solution)/shard_map/mqp,ipojqc->ijmco/dot_general | solution.py:145
  301.0 14.3 %copy.167 = bf16[2,1,64,8,2880]{4,3,2,0,1:T(8,128)(2,1)} copy(bf16[2,1,64,8,2880]{2,4,3,1,0:T(8,128)(2,1)} %fusion.43) | data formatting | bytes 11796480 | tf_op jit(solution)/shard_map/concatenate | solution.py:57
  315.3 4.6 %fusion.44 = bf16[256,1024]{1,0:T(8,128)(2,1)S(1)} fusion(bf16[2880,256]{1,0:T(8,128)(2,1)S(1)} %bitcast.326, bf16[1024,2880]{1,0:T(8,128)(2,1)} %bitcast.319, f32[1024,256]{0,1:T(8,128)S(1)} %copy-done.7), kind=kOutput, calls=%fused_computation.86 | convolution fusion | flops 1512308736 | bytes 8945664 | tf_op jit(solution)/shard_map/dot_general | solution.py:149
  320.0 8.6 %fusion.126 = f32[8,32,3,3,10,32]{5,1,4,3,2,0:T(8,128)S(1)} fusion(bf16[8,32,1024,1,1,1]{2,1,5,4,3,0:T(8,128)(2,1)S(1)} %bitcast.336, bf16[3,3,10,32,1024,1]{4,3,2,1,0,5:T(8,128)(2,1)} %bitcast.320), kind=kOutput, calls=%fused_computation.193 | convolution fusion | flops 1509949440 | bytes 9371648 | tf_op jit(solution)/shard_map/dot_general | solution.py:153
  328.7 18.2 %fusion.48 = f32[3,3,3,32,32]{3,2,1,0,4:T(4,128)S(1)} fusion(f32[8,32,3,3,10,32]{5,1,4,3,2,0:T(8,128)S(1)} %fusion.126), kind=kOutput, calls=%fused_computation.88 | convolution fusion | flops 26542560 | bytes 3059712 | tf_op jit(solution)/shard_map/mqp,poijqc->ijmco/dot_general | solution.py:157
  349.4 7.1 %collective-permute-done.7 = f32[55328]{0:T(1024)S(1)} collective-permute-done((f32[55328]{0:T(1024)S(1)}, f32[55328]{0:T(1024)S(1)}, u32[]{:S(2)}, u32[]{:S(2)}) %collective-permute-start.7) | collective-permute-done | bytes 221344 | tf_op jit(solution)/shard_map/ppermute | solution.py:69
  357.0 12.0 %collective-permute-done.8 = f32[55328]{0:T(1024)S(1)} collective-permute-done((f32[55328]{0:T(1024)S(1)}, f32[55328]{0:T(1024)S(1)}, u32[]{:S(2)}, u32[]{:S(2)}) %collective-permute-start.8) | collective-permute-done | bytes 221344 | tf_op jit(solution)/shard_map/ppermute | solution.py:69
  369.0 7.4 %collective-permute-done.9 = f32[55328]{0:T(1024)S(1)} collective-permute-done((f32[55328]{0:T(1024)S(1)}, f32[55328]{0:T(1024)S(1)}, u32[]{:S(2)}, u32[]{:S(2)}) %collective-permute-start.9) | collective-permute-done | bytes 221344 | tf_op jit(solution)/shard_map/ppermute | solution.py:69
  376.6 6.6 %collective-permute-done.10 = f32[55328]{0:T(1024)S(1)} collective-permute-done((f32[55328]{0:T(1024)S(1)}, f32[55328]{0:T(1024)S(1)}, u32[]{:S(2)}, u32[]{:S(2)}) %collective-permute-start.10) | collective-permute-done | bytes 221344 | tf_op jit(solution)/shard_map/ppermute | solution.py:69
  (152 shorter events, 110.1 us)
Async XLA Ops:
  0.6 1.6 copy-start
  0.6 3.5 copy-start.12
  4.1 14.1 %copy-start.9 = (bf16[3,3,3,32,32]{4,3,2,1,0:T(8,128)(2,1)S(1)}, bf16[3,3,3,32,32]{4,3,2,1,0:T(8,128)(2,1)}, u32[]{:S(2)}) copy-start(bf16[3,3,3,32,32]{4,3,2,1,0:T(8,128)(2,1)} %param.14) | copy-start | bytes 165892
  10.9 111.8 %collective-permute-start.1 = (bf16[2,1,64,64,32]{2,4,3,0,1:T(8,128)(2,1)}, bf16[2,1,64,64,32]{2,4,3,0,1:T(8,128)(2,1)}, u32[]{:S(2)}, u32[]{:S(2)}) collective-permute-start(bf16[2,1,64,64,32]{2,4,3,0,1:T(8,128)(2,1)} %copy.137), channel_id=1, source_target_pairs={{8,0},{16,8},{24,16},{9,1},{17,9},{25,17},{10,2},{18,10},{26,18},{... | collective-permute-start | bytes 1572872 | tf_op jit(solution)/shard_map/ppermute | solution.py:21
  14.2 108.5 %collective-permute-start = (bf16[2,1,64,64,32]{2,4,3,0,1:T(8,128)(2,1)}, bf16[2,1,64,64,32]{2,4,3,0,1:T(8,128)(2,1)}, u32[]{:S(2)}, u32[]{:S(2)}) collective-permute-start(bf16[2,1,64,64,32]{2,4,3,0,1:T(8,128)(2,1)} %copy.137), channel_id=1, source_target_pairs={{0,8},{8,16},{16,24},{1,9},{9,17},{17,25},{2,10},{10,18},{18,26},{... | collective-permute-start | bytes 1572872 | tf_op jit(solution)/shard_map/ppermute | solution.py:20
  52.7 21.5 %copy-start.10 = (bf16[3,3,3,32,32]{4,3,2,1,0:T(8,128)(2,1)S(1)}, bf16[3,3,3,32,32]{4,3,2,1,0:T(8,128)(2,1)}, u32[]{:S(2)}) copy-start(bf16[3,3,3,32,32]{4,3,2,1,0:T(8,128)(2,1)} %param.13) | copy-start | bytes 165892
  116.9 5.7 %copy-start.13 = (bf16[32]{0:T(256)(128)(2,1)S(1)}, bf16[32]{0:T(256)(128)(2,1)}, u32[]{:S(2)}) copy-start(bf16[32]{0:T(256)(128)(2,1)} %param.15) | copy-start | bytes 196
  177.7 1.6 copy-start.3
  179.3 15.9 %copy-start.4 = (bf16[2,64,64,32]{2,1,3,0:T(8,128)(2,1)S(1)}, bf16[2,64,64,32]{2,1,3,0:T(8,128)(2,1)}, u32[]{:S(2)}) copy-start(bf16[2,64,64,32]{2,1,3,0:T(8,128)(2,1)} %reshape.706) | copy-start | bytes 1572868
  188.1 22.1 %collective-permute-start.3 = (f32[2,1,64,64]{2,3,0,1:T(8,128)S(1)}, f32[2,1,64,64]{2,3,0,1:T(8,128)S(1)}, u32[]{:S(2)}, u32[]{:S(2)}) collective-permute-start(f32[2,1,64,64]{2,3,0,1:T(8,128)S(1)} %bitcast.331), channel_id=1, source_target_pairs={{8,0},{16,8},{24,16},{9,1},{17,9},{25,17},{10,2},{18,10},{26,18},{... | collective-permute-start | bytes 98312 | tf_op jit(solution)/shard_map/ppermute | solution.py:21
  192.6 17.6 %collective-permute-start.2 = (f32[2,1,64,64]{2,3,0,1:T(8,128)S(1)}, f32[2,1,64,64]{2,3,0,1:T(8,128)S(1)}, u32[]{:S(2)}, u32[]{:S(2)}) collective-permute-start(f32[2,1,64,64]{2,3,0,1:T(8,128)S(1)} %bitcast.332), channel_id=1, source_target_pairs={{0,8},{8,16},{16,24},{1,9},{9,17},{17,25},{2,10},{10,18},{18,26},{... | collective-permute-start | bytes 98312 | tf_op jit(solution)/shard_map/ppermute | solution.py:20
  214.3 6.6 %collective-permute-start.5 = (bf16[2,1,64,64]{2,3,0,1:T(8,128)(2,1)S(1)}, bf16[2,1,64,64]{2,3,0,1:T(8,128)(2,1)S(1)}, u32[]{:S(2)}, u32[]{:S(2)}) collective-permute-start(bf16[2,1,64,64]{2,3,0,1:T(8,128)(2,1)S(1)} %copy.162), channel_id=1, source_target_pairs={{8,0},{16,8},{24,16},{9,1},{17,9},{25,17},{10,2},{18,10},{26,18},{... | collective-permute-start | bytes 49160 | tf_op jit(solution)/shard_map/ppermute | solution.py:21
  218.5 6.7 %collective-permute-start.4 = (bf16[2,1,64,64]{2,3,0,1:T(8,128)(2,1)S(1)}, bf16[2,1,64,64]{2,3,0,1:T(8,128)(2,1)S(1)}, u32[]{:S(2)}, u32[]{:S(2)}) collective-permute-start(bf16[2,1,64,64]{2,3,0,1:T(8,128)(2,1)S(1)} %copy.162), channel_id=1, source_target_pairs={{0,8},{8,16},{16,24},{1,9},{9,17},{17,25},{2,10},{10,18},{18,26},{... | collective-permute-start | bytes 49160 | tf_op jit(solution)/shard_map/ppermute | solution.py:20
  226.6 1.7 copy-start.2
  236.3 3.3 copy-start.14
  267.6 17.4 %copy-start.6 = (bf16[2,3,64,7,32]{2,4,3,1,0:T(8,128)(2,1)S(1)}, bf16[2,3,64,7,32]{2,4,3,1,0:T(8,128)(2,1)}, u32[]{:S(2)}) copy-start(bf16[2,3,64,7,32]{2,4,3,1,0:T(8,128)(2,1)} %get-tuple-element.28) | copy-start | bytes 516100
  267.6 17.4 %copy-start.11 = (bf16[2,3,64,1,32]{2,4,3,1,0:T(8,128)(2,1)S(1)}, bf16[2,3,64,1,32]{2,4,3,1,0:T(8,128)(2,1)}, u32[]{:S(2)}) copy-start(bf16[2,3,64,1,32]{2,4,3,1,0:T(8,128)(2,1)} %get-tuple-element.26) | copy-start | bytes 73732
  301.0 14.3 %copy-start.5 = (bf16[3,3,320,256]{3,2,1,0:T(8,128)(2,1)S(1)}, bf16[3,3,320,256]{3,2,1,0:T(8,128)(2,1)}, u32[]{:S(2)}) copy-start(bf16[3,3,320,256]{3,2,1,0:T(8,128)(2,1)} %get-tuple-element.38) | copy-start | bytes 4423684
  301.0 14.3 %copy-start.7 = (f32[1024,256]{0,1:T(8,128)S(1)}, f32[1024,256]{0,1:T(8,128)}, u32[]{:S(2)}) copy-start(f32[1024,256]{0,1:T(8,128)} %get-tuple-element.50) | copy-start | bytes 3145732
  328.6 18.6 %copy-start.8 = (f32[27648]{0:T(1024)S(1)}, f32[27648]{0:T(1024)}, u32[]{:S(2)}) copy-start(f32[27648]{0:T(1024)} %reshape.722) | copy-start | bytes 331780
  328.6 56.9 %copy-start.1 = (bf16[1,64,128,128]{3,2,1,0:T(8,128)(2,1)S(1)}, bf16[1,64,128,128]{3,2,1,0:T(8,128)(2,1)}, u32[]{:S(2)}) copy-start(bf16[1,64,128,128]{3,2,1,0:T(8,128)(2,1)} %param.10) | copy-start | bytes 6291460
  347.3 1.5 collective-permute-start.6
  348.9 7.6 %collective-permute-start.7 = (f32[55328]{0:T(1024)S(1)}, f32[55328]{0:T(1024)S(1)}, u32[]{:S(2)}, u32[]{:S(2)}) collective-permute-start(f32[55328]{0:T(1024)S(1)} %fusion.115), channel_id=1, source_target_pairs={{0,2},{1,3},{2,0},{3,1},{4,6},{5,7},{6,4},{7,5},{8,10},{9,11},{10,... | collective-permute-start | bytes 663944 | tf_op jit(solution)/shard_map/ppermute | solution.py:69
  356.5 12.4 %collective-permute-start.8 = (f32[55328]{0:T(1024)S(1)}, f32[55328]{0:T(1024)S(1)}, u32[]{:S(2)}, u32[]{:S(2)}) collective-permute-start(f32[55328]{0:T(1024)S(1)} %add.88), channel_id=1, source_target_pairs={{0,4},{1,5},{2,6},{3,7},{4,0},{5,1},{6,2},{7,3},{8,12},{9,13},{10,... | collective-permute-start | bytes 663944 | tf_op jit(solution)/shard_map/ppermute | solution.py:69
  369.0 7.5 %collective-permute-start.9 = (f32[55328]{0:T(1024)S(1)}, f32[55328]{0:T(1024)S(1)}, u32[]{:S(2)}, u32[]{:S(2)}) collective-permute-start(f32[55328]{0:T(1024)S(1)} %add.89), channel_id=1, source_target_pairs={{0,8},{8,0},{16,24},{24,16},{1,9},{9,1},{17,25},{25,17},{2,10},{10... | collective-permute-start | bytes 663944 | tf_op jit(solution)/shard_map/ppermute | solution.py:69
  376.5 6.6 %collective-permute-start.10 = (f32[55328]{0:T(1024)S(1)}, f32[55328]{0:T(1024)S(1)}, u32[]{:S(2)}, u32[]{:S(2)}) collective-permute-start(f32[55328]{0:T(1024)S(1)} %add.90), channel_id=1, source_target_pairs={{0,16},{8,24},{16,0},{24,8},{1,17},{9,25},{17,1},{25,9},{2,18},{10... | collective-permute-start | bytes 663944 | tf_op jit(solution)/shard_map/ppermute | solution.py:69
